TPU v7x, 32 devices: a whole 2x2x4 slice. The times are simulated.
32 devices in a mesh: seq: 2 (over x), mp: 4 (over z), dp: 4 (over y, core).
Axes of the slice: x: 2, y: 2, z: 4, core: 2. Of those that a mesh axis runs over, the one named last changes fastest.
Arguments:
- features: bfloat16 [4, 2048, 768], P('dp', 'seq'), may hold values from -6 to 6
- conv_weight: bfloat16 [5, 768, 768], P(None, 'mp'), may hold values from -0.09375 to 0.09375
- keep: int32 [4], P('dp'), may hold values 0 or 1
- tiles: int32 [4, 2, 2, 2], P('dp'), may hold values from 0 to 63, as said below
- counts: int32 [4, 2], P('dp'), may hold values from 0 to 2, as said below
- targets: float32 [4, 2, 2, 1024], P('dp', 'seq'), may hold values from -6 to 6
Outputs:
- conv_grad: float32 [5, 768, 768], P(None, 'mp', ('seq', 'dp'))
Inputs may be any that keep to these rules, and one draw needn't show every extreme that they name: `tiles`: entries are block numbers of 32 positions in a sequence. For every sequence and owner, listing the 2 row blocks and then the 2 column blocks, exactly 2 of these 4 entries lie in the positions of each index of seq. Each owner's live slots are its first counts slots; in every sequence some owner has all 2 slots live.
All inputs are finite; a program needn't handle non-finite values. No bound on the sum of `keep` on one device may be relied on, other than what follows from the above.
Results may differ from a plain program's by a relative error of at most 0.0015.
Values may be sent and summed in bfloat16 or wider, within the bound.
No kernel may reach another device: no remote copies, remote signals or barrier semaphores. Data moves between devices by JAX's collectives and lax.ppermute only.
A program may use at most 64 MiB of HBM per device.

v0:
```python
import math
import jax
import jax.numpy as jnp
from jax import lax
from jax.sharding import PartitionSpec as P

TB = 32
PER = 2


def extended(cells, sides, width):
    for axis, dim in sides:
        count = lax.axis_size(axis)
        ends = count - 1
        head = lax.slice_in_dim(cells, 0, width, axis=dim)
        tail = lax.slice_in_dim(cells, cells.shape[dim] - width, cells.shape[dim], axis=dim)
        cells = jnp.concatenate(
            [
                lax.ppermute(tail, axis, [(i, (i + 1) % count) for i in range(ends)]),
                cells,
                lax.ppermute(head, axis, [((i + 1) % count, i) for i in range(ends)]),
            ],
            axis=dim,
        )
    return cells


def take_rows(source_array, index_array):
    return jax.vmap(lambda table, picked: table[picked])(source_array, index_array)


def conv_apply(padded, weight, length):
    total = jnp.einsum(
        "mbi,oi->mbo", padded[:, 0:length], weight[0], preferred_element_type=jnp.float32
    )
    for offset in range(1, weight.shape[0]):
        total = total + jnp.einsum(
            "mbi,oi->mbo",
            padded[:, offset : offset + length],
            weight[offset],
            preferred_element_type=jnp.float32,
        )
    return total


def weight_term(padded, dconv, length, taps):
    return jnp.stack(
        [
            jnp.einsum(
                "mbi,mbo->oi",
                padded[:, offset : offset + length],
                dconv,
                preferred_element_type=jnp.float32,
            )
            for offset in range(taps)
        ]
    )


def dense_path(features, conv_weight, keep, tiles, counts, targets):
    members, length, width = features.shape
    taps = conv_weight.shape[0]
    narrow = conv_weight.shape[1]
    seq_count = lax.axis_size("seq")
    my_index = lax.axis_index("seq")
    my_part = lax.axis_index("mp")
    x_float = features.astype(jnp.float32)
    activations = jax.nn.gelu(x_float).astype(jnp.bfloat16)
    padded = extended(activations, (("seq", 1),), 2)
    scaling = 1.25 * keep.astype(jnp.float32)
    conv_out = conv_apply(padded, conv_weight, length)
    x_local = lax.dynamic_slice_in_dim(x_float, my_part * narrow, narrow, 2)
    mixed_out = (x_local + scaling[:, None, None] * conv_out).astype(jnp.bfloat16)
    capacity = tiles.shape[2]
    n_sides = 2 * capacity
    per_block = length // TB
    sides = jnp.concatenate([tiles[..., 0], tiles[..., 1]], axis=-1)
    side_source = sides // per_block
    side_local = sides % per_block
    own_sides = lax.dynamic_index_in_dim(sides, my_index, 1, keepdims=False)
    own_source = own_sides // per_block
    before = jnp.arange(n_sides)[None, :] < jnp.arange(n_sides)[:, None]
    same_source = own_source[:, :, None] == own_source[:, None, :]
    rank_within = jnp.sum(jnp.logical_and(same_source, before[None]), axis=-1)
    slot_index = own_source * PER + rank_within
    held_here = side_source == my_index
    held_order = jnp.cumsum(held_here.astype(jnp.int32), axis=-1) - 1
    picks = jnp.stack(
        [
            jnp.sum(
                jnp.where(jnp.logical_and(held_here, held_order == position), side_local, 0),
                axis=-1,
            )
            for position in range(PER)
        ],
        axis=-1,
    )
    blocks = mixed_out.reshape(members, per_block, TB, narrow)
    whole = lax.all_gather(blocks, "seq", axis=1, tiled=True)
    side_rows = take_rows(whole, own_sides)
    row_side = side_rows[:, :capacity]
    col_side = side_rows[:, capacity:]
    partial_tiles = jnp.einsum(
        "mcid,mcjd->mcij", row_side, col_side, preferred_element_type=jnp.float32
    )
    predicted = lax.psum(partial_tiles, "mp") / math.sqrt(width)
    target_tiles = targets[:, 0].reshape(members, capacity, TB, TB)
    own_count = lax.dynamic_index_in_dim(counts, my_index, 1, keepdims=False)
    live_mask = (jnp.arange(capacity)[None, :] < own_count[:, None]).astype(jnp.float32)
    n_live = jnp.sum(counts, axis=-1).astype(jnp.float32)
    dpredicted = (
        2.0
        / math.sqrt(width)
        * live_mask[:, :, None, None]
        * (predicted - target_tiles)
        / n_live[:, None, None, None]
    )
    row_float = row_side.astype(jnp.float32)
    col_float = col_side.astype(jnp.float32)
    drow = jnp.einsum("mcij,mcjd->mcid", dpredicted, col_float, precision=lax.Precision.HIGHEST)
    dcol = jnp.einsum("mcij,mcid->mcjd", dpredicted, row_float, precision=lax.Precision.HIGHEST)
    dside = jnp.concatenate([drow, dcol], axis=1).astype(jnp.bfloat16)
    inverse = jnp.argsort(slot_index, axis=-1)
    outgoing_grads = take_rows(dside, inverse).reshape(members, seq_count, PER, TB, narrow)
    returned = lax.all_to_all(outgoing_grads, "seq", split_axis=1, concat_axis=1, tiled=True)
    selector = (
        picks.reshape(members, seq_count * PER)[:, :, None] == jnp.arange(per_block)[None, None, :]
    ).astype(jnp.bfloat16)
    dmixed = jnp.einsum(
        "mkn,mktd->mntd",
        selector,
        returned.reshape(members, seq_count * PER, TB, narrow),
        preferred_element_type=jnp.float32,
    ).reshape(members, length, narrow)
    dconv = (scaling[:, None, None] * dmixed).astype(jnp.bfloat16)
    weight_local = weight_term(padded, dconv, length, taps)
    return lax.psum_scatter(weight_local, ("seq", "dp"), scatter_dimension=2, tiled=True)


def axis_sum(value, axis):
    count = lax.axis_size(axis)
    total = value
    for shift in range(1, count):
        total = total + lax.ppermute(value, axis, [(i, (i + shift) % count) for i in range(count)])
    return total


def sparse_path(features, conv_weight, keep, tiles, counts, targets):
    _, length, width = features.shape
    taps, narrow, _ = conv_weight.shape
    halo = taps // 2
    span = TB + 2 * halo
    owners, capacity = (tiles.shape[1], tiles.shape[2])
    n_sides = 2 * capacity
    per_block = length // TB
    seq_count = lax.axis_size("seq")
    groups = lax.axis_size("dp")
    peers = seq_count * groups
    held = owners * PER
    cols = width // peers
    my_index = lax.axis_index("seq")
    my_part = lax.axis_index("mp")
    small = jnp.concatenate([tiles.reshape(-1), counts.reshape(-1), keep.reshape(-1)]).astype(
        jnp.float32
    )
    bundle = jnp.concatenate([targets.reshape(-1), small])
    gathered = lax.all_gather(bundle, ("seq", "dp")).reshape(seq_count, groups, -1)
    n_targets = capacity * TB * TB
    n_tiles = owners * capacity * 2
    meta = gathered[0, :, n_targets:].astype(jnp.int32)
    tiles_all = meta[:, :n_tiles].reshape(groups, owners, capacity, 2)
    counts_all = meta[:, n_tiles : n_tiles + owners]
    keep_all = meta[:, n_tiles + owners]
    targets_all = gathered[:, :, :n_targets]
    sides = jnp.concatenate([tiles_all[..., 0], tiles_all[..., 1]], axis=-1)
    source = sides // per_block
    local = sides % per_block
    before = jnp.arange(n_sides)[None, :] < jnp.arange(n_sides)[:, None]
    same_source = source[..., :, None] == source[..., None, :]
    rank = jnp.sum(jnp.logical_and(same_source, before), axis=-1)
    slot = (
        (source * groups + jnp.arange(groups)[:, None, None]) * held
        + jnp.arange(owners)[None, :, None] * PER
        + rank
    )
    mine = lax.dynamic_index_in_dim(
        jnp.stack([source, local, rank], 0), lax.axis_index("dp"), 1, keepdims=False
    )
    held_here = mine[0] == my_index
    picks = jnp.stack(
        [
            jnp.sum(jnp.where(jnp.logical_and(held_here, mine[2] == r), mine[1], 0), axis=-1)
            for r in range(PER)
        ],
        axis=-1,
    ).reshape(held)
    cells = features[0]
    ends = seq_count - 1
    head = lax.ppermute(cells[length - halo :], "seq", [(i, i + 1) for i in range(ends)])
    tail = lax.ppermute(cells[:halo], "seq", [(i + 1, i) for i in range(ends)])
    rows = picks[:, None] * TB - halo + jnp.arange(span)[None, :]
    inside = jnp.take(cells, jnp.clip(rows, 0, length - 1), axis=0)
    edge_rows = jnp.concatenate([head, tail], axis=0)
    edge_index = jnp.where(rows < 0, rows + halo, rows - length + halo)
    outside = jnp.take(edge_rows, jnp.clip(edge_index, 0, 2 * halo - 1), axis=0)
    in_range = jnp.logical_and(rows >= 0, rows < length)
    windows = jnp.where(in_range[..., None], inside, outside)
    x_float = windows.astype(jnp.float32)
    act = jax.nn.gelu(x_float).astype(jnp.bfloat16)
    conv_out = jnp.einsum(
        "hti,oi->hto", act[:, 0:TB], conv_weight[0], preferred_element_type=jnp.float32
    )
    for offset in range(1, taps):
        conv_out = conv_out + jnp.einsum(
            "hti,oi->hto",
            act[:, offset : offset + TB],
            conv_weight[offset],
            preferred_element_type=jnp.float32,
        )
    scaling = 1.25 * keep_all.astype(jnp.float32)
    my_scale = lax.dynamic_index_in_dim(scaling, lax.axis_index("dp"), 0, keepdims=False)
    x_part = lax.dynamic_slice_in_dim(x_float[:, halo : halo + TB], my_part * narrow, narrow, 2)
    mixed = (x_part + my_scale * conv_out).astype(jnp.bfloat16)
    act_cut = act.reshape(held, span, peers, cols).transpose(2, 0, 1, 3).reshape(peers, -1)
    mixed_rep = jnp.broadcast_to(mixed.reshape(1, -1), (peers, held * TB * narrow))
    outgoing = jnp.concatenate([mixed_rep, act_cut], axis=1)
    incoming = lax.all_to_all(outgoing, ("seq", "dp"), 0, 0, tiled=True)
    mixed_in = incoming[:, : held * TB * narrow].reshape(peers * held, TB, narrow)
    act_in = incoming[:, held * TB * narrow :].reshape(peers * held, span, cols)
    side_rows = jnp.take(mixed_in, slot, axis=0)
    row_side = side_rows[:, :, :capacity]
    col_side = side_rows[:, :, capacity:]
    partial_tiles = jnp.einsum(
        "qocid,qocjd->qocij", row_side, col_side, preferred_element_type=jnp.float32
    )
    predicted = axis_sum(partial_tiles, "mp") / math.sqrt(width)
    target_tiles = targets_all.reshape(seq_count, groups, capacity, TB, TB).transpose(1, 0, 2, 3, 4)
    live_mask = (jnp.arange(capacity)[None, None, :] < counts_all[:, :, None]).astype(jnp.float32)
    n_live = jnp.sum(counts_all, axis=-1).astype(jnp.float32)
    dpredicted = (
        2.0
        / math.sqrt(width)
        * live_mask[..., None, None]
        * (predicted - target_tiles)
        / n_live[:, None, None, None, None]
    )
    row_float = row_side.astype(jnp.float32)
    col_float = col_side.astype(jnp.float32)
    drow = jnp.einsum("qocij,qocjd->qocid", dpredicted, col_float, precision=lax.Precision.HIGHEST)
    dcol = jnp.einsum("qocij,qocid->qocjd", dpredicted, row_float, precision=lax.Precision.HIGHEST)
    grads = jnp.concatenate([drow, dcol], axis=2).astype(jnp.bfloat16).astype(jnp.float32)
    grads = grads.reshape(groups, owners * n_sides, TB, narrow)
    flat_sides = sides.reshape(groups, owners * n_sides)
    same_block = flat_sides[:, :, None] == flat_sides[:, None, :]
    total = jnp.sum(jnp.where(same_block[..., None, None], grads[:, None], 0.0), axis=2)
    earlier = jnp.arange(owners * n_sides)[None, :] < jnp.arange(owners * n_sides)[:, None]
    first = jnp.logical_not(jnp.any(jnp.logical_and(same_block, earlier[None]), axis=-1))
    dconv = (scaling[:, None, None, None] * total).astype(jnp.bfloat16)
    dconv = jnp.where(first[..., None, None], dconv, jnp.zeros_like(dconv))
    act_sides = jnp.take(act_in, slot.reshape(groups, owners * n_sides), axis=0)
    return jnp.stack(
        [
            jnp.einsum(
                "qato,qati->oi",
                dconv,
                act_sides[:, :, offset : offset + TB],
                preferred_element_type=jnp.float32,
            )
            for offset in range(taps)
        ]
    )


def per_device(features, conv_weight, keep, tiles, counts, targets):
    members, length, _ = features.shape
    owners, capacity = (tiles.shape[1], tiles.shape[2])
    fits = members == 1 and targets.shape[1] == 1 and (2 * owners * capacity * TB <= length)
    if fits:
        return sparse_path(features, conv_weight, keep, tiles, counts, targets)
    return dense_path(features, conv_weight, keep, tiles, counts, targets)


def solution(mesh):
    placed = (
        P("dp", "seq", None),
        P(None, "mp", None),
        P("dp"),
        P("dp", None, None, None),
        P("dp", None),
        P("dp", "seq", None, None),
    )
    return jax.shard_map(
        per_device,
        mesh=mesh,
        in_specs=placed,
        out_specs=P(None, "mp", ("seq", "dp")),
        check_vma=False,
    )
```

profile of v0, /device:TPU:0, one launch (start us, length us, event | category | flops | bytes accessed | tf_op | source)
XLA Modules:
  0.0 141.5 jit_solution(4417940106494104526)
XLA Ops:
  6.5 0.7 slice_bitcast_fusion.1
  7.3 4.8 %collective-permute-start = (bf16[2,768]{1,0:T(2,128)(2,1)S(1)}, bf16[2,768]{1,0:T(2,128)(2,1)S(1)}, u32[]{:S(2)}, u32[]{:S(2)}) collective-permute-start(bf16[2,768]{1,0:T(2,128)(2,1)S(1)} %get-tuple-element.11), channel_id=1, source_target_pairs={{0,16},{1,17},{2,18},{3,19},{4,20},{5,21},{6,22},{7,23},{8,24},{9,... | collective-permute-start | bytes 9224 | tf_op jit(solution)/shard_map/ppermute | solution.py:199
  12.1 1.3 collective-permute-start.1
  14.1 0.8 reshape.924
  14.8 0.7 copy.140
  15.5 1.2 dynamic-slice.1
  17.4 0.7 add_convert_fusion
  18.3 0.6 copy-done
  19.2 51.9 %all-reduce.3.cloned.1.call-done = f32[16472]{0:T(1024)} async-done(((f32[16472]{0:T(1024)}), f32[16472]{0:T(1024)}) %all-reduce.3.cloned.1.call-update) | async-done | bytes 65904
  71.1 1.0 reshape.926
  74.4 2.6 %gather_fusion = bf16[144,768]{1,0:T(8,128)(2,1)S(1)} fusion(bf16[1024,768]{1,0:T(8,128)(2,1)} %bitcast.114, s32[1024]{0:T(1024)S(1)} %pad_clamp_fusion.3), kind=kCustom, calls=%fused_computation | custom fusion | bytes 442944 | tf_op jit(solution)/shard_map/jit(_take)/gather | solution.py:202
  77.5 0.9 gather_fusion.1
  78.9 0.5 constant_dynamic-slice_fusion
  80.4 0.4 fusion.23
  81.6 0.9 copy-done.2
  83.6 0.9 fusion.2
  84.8 0.5 broadcast.811
  85.3 1.1 reduce.4
  86.4 1.0 reshape.990
  87.4 3.9 %all-to-all-start = ((bf16[8,2,19200]{2,1,0:T(2,128)(2,1)}), bf16[8,2,19200]{2,1,0:T(2,128)(2,1)S(1)}, u32[]{:S(2)}, u32[]{:S(2)}) async-start(bf16[8,2,19200]{2,1,0:T(2,128)(2,1)} %reshape.990), calls=%async_computation | async-start | bytes 1228800 | tf_op jit(solution)/shard_map/all_to_all | solution.py:227
  91.4 9.7 %all-to-all-done = bf16[8,2,19200]{2,1,0:T(2,128)(2,1)S(1)} async-done(((bf16[8,2,19200]{2,1,0:T(2,128)(2,1)}), bf16[8,2,19200]{2,1,0:T(2,128)(2,1)S(1)}, u32[]{:S(2)}, u32[]{:S(2)}) %all-to-all-start) | async-done | bytes 614432 | tf_op jit(solution)/shard_map/all_to_all | solution.py:227
  101.1 0.5 reshape.991
  101.7 0.6 reshape.929
  102.4 0.6 gather_fusion.2
  103.3 3.4 %collective-permute-start.4 = (f32[4,2,2,32,32]{4,3,2,1,0:T(8,128)S(1)}, f32[4,2,2,32,32]{4,3,2,1,0:T(8,128)S(1)}, u32[]{:S(2)}, u32[]{:S(2)}) collective-permute-start(f32[4,2,2,32,32]{4,3,2,1,0:T(8,128)S(1)} %fusion.50), channel_id=1, source_target_pairs={{0,12},{4,0},{8,4},{12,8},{1,13},{5,1},{9,5},{13,9},{2,14},{6,2},{... | collective-permute-start | bytes 196616 | tf_op jit(solution)/shard_map/ppermute | solution.py:144
  106.7 1.1 collective-permute-start.2
  108.2 0.6 gather_fusion.3
  108.9 4.5 %collective-permute-done.4 = f32[4,2,2,32,32]{4,3,2,1,0:T(8,128)S(1)} collective-permute-done((f32[4,2,2,32,32]{4,3,2,1,0:T(8,128)S(1)}, f32[4,2,2,32,32]{4,3,2,1,0:T(8,128)S(1)}, u32[]{:S(2)}, u32[]{:S(2)}) %collective-permute-start.4) | collective-permute-done | bytes 65568 | tf_op jit(solution)/shard_map/ppermute | solution.py:144
  113.5 15.5 %collective-permute-done.3 = f32[4,2,2,32,32]{4,3,2,1,0:T(8,128)S(1)} collective-permute-done((f32[4,2,2,32,32]{4,3,2,1,0:T(8,128)S(1)}, f32[4,2,2,32,32]{4,3,2,1,0:T(8,128)S(1)}, u32[]{:S(2)}, u32[]{:S(2)}) %collective-permute-start.3) | collective-permute-done | bytes 65568 | tf_op jit(solution)/shard_map/ppermute | solution.py:144
  130.1 1.4 select_reduce_fusion
  133.0 0.8 copy-done.3
  133.7 1.0 fusion.3
  (94 shorter events, 10.0 us)
Async XLA Ops:
  6.5 64.6 %all-reduce.3.cloned.1.call-start = ((), (), s32[]{:S(2)}) async-start(), calls=%async_computation.1 | async-start | bytes 139264
  7.3 11.9 %collective-permute-start = (bf16[2,768]{1,0:T(2,128)(2,1)S(1)}, bf16[2,768]{1,0:T(2,128)(2,1)S(1)}, u32[]{:S(2)}, u32[]{:S(2)}) collective-permute-start(bf16[2,768]{1,0:T(2,128)(2,1)S(1)} %get-tuple-element.11), channel_id=1, source_target_pairs={{0,16},{1,17},{2,18},{3,19},{4,20},{5,21},{6,22},{7,23},{8,24},{9,... | collective-permute-start | bytes 9224 | tf_op jit(solution)/shard_map/ppermute | solution.py:199
  12.1 7.1 %collective-permute-start.1 = (bf16[2,768]{1,0:T(2,128)(2,1)S(1)}, bf16[2,768]{1,0:T(2,128)(2,1)S(1)}, u32[]{:S(2)}, u32[]{:S(2)}) collective-permute-start(bf16[2,768]{1,0:T(2,128)(2,1)S(1)} %get-tuple-element.12), channel_id=1, source_target_pairs={{16,0},{17,1},{18,2},{19,3},{20,4},{21,5},{22,6},{23,7},{24,8},{25... | collective-permute-start | bytes 9224 | tf_op jit(solution)/shard_map/ppermute | solution.py:200
  18.3 0.6 copy-start
  72.1 4.9 %copy-start.1 = (f32[2,4,2059]{2,1,0:T(4,128)}, f32[2,4,2059]{2,1,0:T(4,128)S(1)}, u32[]{:S(2)}) copy-start(f32[2,4,2059]{2,1,0:T(4,128)S(1)} %reshape.926) | copy-start | bytes 197668
  77.5 1.3 slice-start
  81.2 1.4 copy-start.2
  87.4 13.7 %all-to-all-start = ((bf16[8,2,19200]{2,1,0:T(2,128)(2,1)}), bf16[8,2,19200]{2,1,0:T(2,128)(2,1)S(1)}, u32[]{:S(2)}, u32[]{:S(2)}) async-start(bf16[8,2,19200]{2,1,0:T(2,128)(2,1)} %reshape.990), calls=%async_computation | async-start | bytes 1228800 | tf_op jit(solution)/shard_map/all_to_all | solution.py:227
  103.3 10.2 %collective-permute-start.4 = (f32[4,2,2,32,32]{4,3,2,1,0:T(8,128)S(1)}, f32[4,2,2,32,32]{4,3,2,1,0:T(8,128)S(1)}, u32[]{:S(2)}, u32[]{:S(2)}) collective-permute-start(f32[4,2,2,32,32]{4,3,2,1,0:T(8,128)S(1)} %fusion.50), channel_id=1, source_target_pairs={{0,12},{4,0},{8,4},{12,8},{1,13},{5,1},{9,5},{13,9},{2,14},{6,2},{... | collective-permute-start | bytes 196616 | tf_op jit(solution)/shard_map/ppermute | solution.py:144
  106.7 22.3 %collective-permute-start.3 = (f32[4,2,2,32,32]{4,3,2,1,0:T(8,128)S(1)}, f32[4,2,2,32,32]{4,3,2,1,0:T(8,128)S(1)}, u32[]{:S(2)}, u32[]{:S(2)}) collective-permute-start(f32[4,2,2,32,32]{4,3,2,1,0:T(8,128)S(1)} %fusion.50), channel_id=1, source_target_pairs={{0,8},{4,12},{8,0},{12,4},{1,9},{5,13},{9,1},{13,5},{2,10},{6,14},... | collective-permute-start | bytes 196616 | tf_op jit(solution)/shard_map/ppermute | solution.py:144
  106.7 22.3 %collective-permute-start.2 = (f32[4,2,2,32,32]{4,3,2,1,0:T(8,128)S(1)}, f32[4,2,2,32,32]{4,3,2,1,0:T(8,128)S(1)}, u32[]{:S(2)}, u32[]{:S(2)}) collective-permute-start(f32[4,2,2,32,32]{4,3,2,1,0:T(8,128)S(1)} %fusion.50), channel_id=1, source_target_pairs={{0,4},{4,8},{8,12},{12,0},{1,5},{5,9},{9,13},{13,1},{2,6},{6,10},{... | collective-permute-start | bytes 196616 | tf_op jit(solution)/shard_map/ppermute | solution.py:144
  132.9 0.8 copy-start.3
Sparse Core Ops, SparseCore 0:
  19.1 51.9 all-reduce.2
where the time goes:
time: 142 us
  waiting for transfers between devices  81.6 us (57%)
  local copies, waits for them, and re-layouts  18.4 us (13%)
  between operations  15.2 us (11%)
  starting transfers between devices  14.5 us (10%)
  other arithmetic  6.7 us (5%)
  matrix products  5.11 us (4%)
    unnamed x2, waiting for transfers between devices  51.9 us
    ppermute x3, waiting for transfers between devices, axis_sum(): lax.ppermute(value, axis, [(i, (i + shift) % count) for i in range(count)])  20 us
    all_to_all x1, waiting for transfers between devices, sparse_path(): incoming = lax.all_to_all(outgoing, ('seq', 'dp'), 0, 0, tiled=True)  9.65 us
    unnamed x14, local copies, waits for them, and re-layouts  5.84 us
    ppermute x1, starting transfers between devices, sparse_path(): lax.ppermute(cells[length - halo:], 'seq', [(i, i + 1) for i in range(end...  4.83 us
    ppermute x3, starting transfers between devices, axis_sum(): lax.ppermute(value, axis, [(i, (i + shift) % count) for i in range(count)])  4.48 us
    all_to_all x1, starting transfers between devices, sparse_path(): incoming = lax.all_to_all(outgoing, ('seq', 'dp'), 0, 0, tiled=True)  3.92 us
    gather x3, local copies, waits for them, and re-layouts, sparse_path(): inside = jnp.take(cells, jnp.clip(rows, 0, length - 1), axis=0)  3.02 us
  transfers between devices with their start and end apart: 7, of which 4 were waited for; matrix products, arithmetic and copies ran while one was open for 4% of the time, Pallas kernels for 0%

commit v1 on v0

--- a/solution.py
+++ b/solution.py
@@ -6,6 +6,18 @@
 
 TB = 32
 PER = 2
+
+
+def split_up(shard, dim, size):
+    shape = shard.shape
+    blocks = shard.reshape(*shape[:dim], size, shape[dim] // size, *shape[dim + 1 :])
+    return jnp.moveaxis(blocks, dim, 0)
+
+
+def joined_along(blocks, dim):
+    lengths = list(blocks.shape[1:])
+    lengths[dim] *= blocks.shape[0]
+    return jnp.moveaxis(blocks, 0, dim).reshape(lengths)
 
 
 def extended(cells, sides, width):
@@ -224,7 +236,14 @@
     act_cut = act.reshape(held, span, peers, cols).transpose(2, 0, 1, 3).reshape(peers, -1)
     mixed_rep = jnp.broadcast_to(mixed.reshape(1, -1), (peers, held * TB * narrow))
     outgoing = jnp.concatenate([mixed_rep, act_cut], axis=1)
-    incoming = lax.all_to_all(outgoing, ("seq", "dp"), 0, 0, tiled=True)
+    peers_2, position_2 = (lax.axis_size(("seq", "dp")), lax.axis_index(("seq", "dp")))
+    tiles_2 = split_up(outgoing, 0, peers_2)
+    outs = [tiles_2[position_2]]
+    for hop in range(1, peers_2):
+        sent = tiles_2[position_2 ^ hop]
+        outs.append(lax.ppermute(sent, ("seq", "dp"), [(i_2, i_2 ^ hop) for i_2 in range(peers_2)]))
+    tiles_2 = jnp.stack(outs)[position_2 ^ jnp.arange(peers_2)]
+    incoming = joined_along(tiles_2, 0)
     mixed_in = incoming[:, : held * TB * narrow].reshape(peers * held, TB, narrow)
     act_in = incoming[:, held * TB * narrow :].reshape(peers * held, span, cols)
     side_rows = jnp.take(mixed_in, slot, axis=0)

time: 142 us -> 146 us (1.028)
  starting transfers between devices: 14.5 us -> 18.3 us
  local copies, waits for them, and re-layouts: 18.4 us -> 20.4 us
    all_to_all x1 -> x0, waiting for transfers between devices: 9.65 us -> none  [sparse_path(): incoming = lax.all_to_all(outgoing, ('seq', 'dp'), 0, 0, tiled=True)]
    ppermute x0 -> x7, waiting for transfers between devices: none -> 8.73 us  [sparse_path(): lax.ppermute(sent, ('seq', 'dp'), [(i_2, i_2 ^ hop) for i_2 in range(peer...]
    ppermute x0 -> x7, starting transfers between devices: none -> 7.68 us  [sparse_path(): lax.ppermute(sent, ('seq', 'dp'), [(i_2, i_2 ^ hop) for i_2 in range(peer...]
    all_to_all x1 -> x0, starting transfers between devices: 3.92 us -> none  [sparse_path(): incoming = lax.all_to_all(outgoing, ('seq', 'dp'), 0, 0, tiled=True)]
    another operation x0 -> x1, local copies, waits for them, and re-layouts: none -> 1.89 us  [sparse_path(): tiles_2 = jnp.stack(outs)[position_2 ^ jnp.arange(peers_2)]]
    unnamed x14 -> x11, local copies, waits for them, and re-layouts: 5.84 us -> 4.3 us
  transfers between devices with their start and end apart: 7 -> 13, of which waited for: 4 -> 6; matrix products, arithmetic and copies ran while one was open for 4% -> 4% of each run, Pallas kernels for 0% -> 0%
where the time goes in v1:
time: 146 us; the launch traced here: 145 us
  waiting for transfers between devices  80.6 us (55%)
  local copies, waits for them, and re-layouts  20.4 us (14%)
  starting transfers between devices  18.3 us (13%)
  between operations  15.3 us (10%)
  other arithmetic  5.59 us (4%)
  matrix products  5.1 us (3%)
    unnamed x2, waiting for transfers between devices  51.9 us
    ppermute x3, waiting for transfers between devices, axis_sum(): lax.ppermute(value, axis, [(i, (i + shift) % count) for i in range(count)])  19.9 us
    ppermute x7, waiting for transfers between devices, sparse_path(): lax.ppermute(sent, ('seq', 'dp'), [(i_2, i_2 ^ hop) for i_2 in range(peer...  8.73 us
    ppermute x7, starting transfers between devices, sparse_path(): lax.ppermute(sent, ('seq', 'dp'), [(i_2, i_2 ^ hop) for i_2 in range(peer...  7.68 us
    ppermute x1, starting transfers between devices, sparse_path(): lax.ppermute(cells[length - halo:], 'seq', [(i, i + 1) for i in range(end...  4.83 us
    ppermute x3, starting transfers between devices, axis_sum(): lax.ppermute(value, axis, [(i, (i + shift) % count) for i in range(count)])  4.5 us
    unnamed x11, local copies, waits for them, and re-layouts  4.3 us
    gather x3, local copies, waits for them, and re-layouts, sparse_path(): inside = jnp.take(cells, jnp.clip(rows, 0, length - 1), axis=0)  3.02 us
  transfers between devices with their start and end apart: 13, of which 6 were waited for; matrix products, arithmetic and copies ran while one was open for 4% of the time, Pallas kernels for 0%

profile of v1, /device:TPU:0, one launch (start us, length us, event | category | flops | bytes accessed | tf_op | source)
XLA Modules:
  0.0 145.2 jit_solution(13322846227891005172)
XLA Ops:
  6.5 0.7 slice_bitcast_fusion.1
  7.3 4.8 %collective-permute-start = (bf16[2,768]{1,0:T(2,128)(2,1)S(1)}, bf16[2,768]{1,0:T(2,128)(2,1)S(1)}, u32[]{:S(2)}, u32[]{:S(2)}) collective-permute-start(bf16[2,768]{1,0:T(2,128)(2,1)S(1)} %get-tuple-element.11), channel_id=1, source_target_pairs={{0,16},{1,17},{2,18},{3,19},{4,20},{5,21},{6,22},{7,23},{8,24},{9,... | collective-permute-start | bytes 9224 | tf_op jit(solution)/shard_map/ppermute | solution.py:211
  12.1 1.3 collective-permute-start.1
  14.1 0.8 reshape.957
  14.8 0.7 copy.93
  15.5 1.2 dynamic-slice.12
  17.4 0.7 add_convert_fusion
  18.3 0.6 copy-done.1
  19.3 51.9 %all-reduce.3.cloned.1.call-done = f32[16472]{0:T(1024)} async-done(((f32[16472]{0:T(1024)}), f32[16472]{0:T(1024)}) %all-reduce.3.cloned.1.call-update) | async-done | bytes 65904
  71.1 1.0 reshape.959
  74.4 2.6 %gather_fusion = bf16[144,768]{1,0:T(8,128)(2,1)S(1)} fusion(bf16[1024,768]{1,0:T(8,128)(2,1)} %bitcast.122, s32[1024]{0:T(1024)S(1)} %pad_clamp_fusion.4), kind=kCustom, calls=%fused_computation | custom fusion | bytes 442944 | tf_op jit(solution)/shard_map/jit(_take)/gather | solution.py:214
  77.6 0.9 gather_fusion.1
  80.9 0.9 copy-done.2
  82.8 0.9 fusion.2
  84.0 1.3 constant_dynamic-slice_fusion
  85.3 2.7 %collective-permute-start.8 = (bf16[1,38400]{1,0:T(2,128)(2,1)S(1)}, bf16[1,38400]{1,0:T(2,128)(2,1)S(1)}, u32[]{:S(2)}, u32[]{:S(2)}) collective-permute-start(bf16[1,38400]{1,0:T(2,128)(2,1)S(1)} %get-tuple-element.13), channel_id=1, source_target_pairs={{0,19},{1,18},{2,17},{3,16},{16,3},{17,2},{18,1},{19,0},{4,23},{5,... | collective-permute-start | bytes 230408 | tf_op jit(solution)/shard_map/ppermute | solution.py:244
  88.0 1.4 collective-permute-start.7
  90.4 0.6 collective-permute-start.5
  91.0 1.4 collective-permute-start.4
  92.4 1.4 collective-permute-start.3
  93.8 3.2 %collective-permute-done.7 = bf16[1,38400]{1,0:T(2,128)(2,1)S(1)} collective-permute-done((bf16[1,38400]{1,0:T(2,128)(2,1)S(1)}, bf16[1,38400]{1,0:T(2,128)(2,1)S(1)}, u32[]{:S(2)}, u32[]{:S(2)}) %collective-permute-start.7) | collective-permute-done | bytes 76832 | tf_op jit(solution)/shard_map/ppermute | solution.py:244
  97.1 1.8 %collective-permute-done.6 = bf16[1,38400]{1,0:T(2,128)(2,1)S(1)} collective-permute-done((bf16[1,38400]{1,0:T(2,128)(2,1)S(1)}, bf16[1,38400]{1,0:T(2,128)(2,1)S(1)}, u32[]{:S(2)}, u32[]{:S(2)}) %collective-permute-start.6) | collective-permute-done | bytes 76832 | tf_op jit(solution)/shard_map/ppermute | solution.py:244
  98.9 3.7 %collective-permute-done.5 = bf16[1,38400]{1,0:T(2,128)(2,1)S(1)} collective-permute-done((bf16[1,38400]{1,0:T(2,128)(2,1)S(1)}, bf16[1,38400]{1,0:T(2,128)(2,1)S(1)}, u32[]{:S(2)}, u32[]{:S(2)}) %collective-permute-start.5) | collective-permute-done | bytes 76832 | tf_op jit(solution)/shard_map/ppermute | solution.py:244
  102.6 1.9 %stack.71 = bf16[8,1,38400]{2,0,1:T(8,128)(2,1)S(1)} concatenate(bf16[1,1,38400]{2,0,1:T(2,128)(2,1)S(1)} %get-tuple-element.20, bf16[1,1,38400]{2,0,1:T(2,128)(2,1)S(1)} %bitcast.132, bf16[1,1,38400]{2,0,1:T(2,128)(2,1)S(1)} %bitcast.131, bf16[1,1,38400]{2,0,1:T(2,128)(2,1)S(1)} %bitcast.130, bf16[1,1,38400]{2,0,1:T(2,128)(2,1)S(1)} %bitcast.129, ...), dimensions={0} | concatenate | bytes 1228800 | tf_op jit(solution)/shard_map/stack | solution.py:245
  104.5 1.0 gather_fusion.2
  107.1 3.4 %collective-permute-start.11 = (f32[4,2,2,32,32]{4,3,2,1,0:T(8,128)S(1)}, f32[4,2,2,32,32]{4,3,2,1,0:T(8,128)S(1)}, u32[]{:S(2)}, u32[]{:S(2)}) collective-permute-start(f32[4,2,2,32,32]{4,3,2,1,0:T(8,128)S(1)} %fusion.50), channel_id=1, source_target_pairs={{0,12},{4,0},{8,4},{12,8},{1,13},{5,1},{9,5},{13,9},{2,14},{6,2},{... | collective-permute-start | bytes 196616 | tf_op jit(solution)/shard_map/ppermute | solution.py:156
  110.5 1.1 collective-permute-start.9
  112.7 4.5 %collective-permute-done.11 = f32[4,2,2,32,32]{4,3,2,1,0:T(8,128)S(1)} collective-permute-done((f32[4,2,2,32,32]{4,3,2,1,0:T(8,128)S(1)}, f32[4,2,2,32,32]{4,3,2,1,0:T(8,128)S(1)}, u32[]{:S(2)}, u32[]{:S(2)}) %collective-permute-start.11) | collective-permute-done | bytes 65568 | tf_op jit(solution)/shard_map/ppermute | solution.py:156
  117.2 15.4 %collective-permute-done.10 = f32[4,2,2,32,32]{4,3,2,1,0:T(8,128)S(1)} collective-permute-done((f32[4,2,2,32,32]{4,3,2,1,0:T(8,128)S(1)}, f32[4,2,2,32,32]{4,3,2,1,0:T(8,128)S(1)}, u32[]{:S(2)}, u32[]{:S(2)}) %collective-permute-start.10) | collective-permute-done | bytes 65568 | tf_op jit(solution)/shard_map/ppermute | solution.py:156
  133.8 1.4 select_reduce_fusion
  136.7 0.8 copy-done.3
  137.4 1.0 fusion.3
  (106 shorter events, 12.8 us)
Async XLA Ops:
  6.5 64.6 %all-reduce.3.cloned.1.call-start = ((), (), s32[]{:S(2)}) async-start(), calls=%async_computation | async-start | bytes 139264
  7.3 12.0 %collective-permute-start = (bf16[2,768]{1,0:T(2,128)(2,1)S(1)}, bf16[2,768]{1,0:T(2,128)(2,1)S(1)}, u32[]{:S(2)}, u32[]{:S(2)}) collective-permute-start(bf16[2,768]{1,0:T(2,128)(2,1)S(1)} %get-tuple-element.11), channel_id=1, source_target_pairs={{0,16},{1,17},{2,18},{3,19},{4,20},{5,21},{6,22},{7,23},{8,24},{9,... | collective-permute-start | bytes 9224 | tf_op jit(solution)/shard_map/ppermute | solution.py:211
  12.1 7.1 %collective-permute-start.1 = (bf16[2,768]{1,0:T(2,128)(2,1)S(1)}, bf16[2,768]{1,0:T(2,128)(2,1)S(1)}, u32[]{:S(2)}, u32[]{:S(2)}) collective-permute-start(bf16[2,768]{1,0:T(2,128)(2,1)S(1)} %get-tuple-element.12), channel_id=1, source_target_pairs={{16,0},{17,1},{18,2},{19,3},{20,4},{21,5},{22,6},{23,7},{24,8},{25... | collective-permute-start | bytes 9224 | tf_op jit(solution)/shard_map/ppermute | solution.py:212
  18.3 0.6 copy-start.1
  80.4 1.4 copy-start.2
  85.3 7.1 %collective-permute-start.8 = (bf16[1,38400]{1,0:T(2,128)(2,1)S(1)}, bf16[1,38400]{1,0:T(2,128)(2,1)S(1)}, u32[]{:S(2)}, u32[]{:S(2)}) collective-permute-start(bf16[1,38400]{1,0:T(2,128)(2,1)S(1)} %get-tuple-element.13), channel_id=1, source_target_pairs={{0,19},{1,18},{2,17},{3,16},{16,3},{17,2},{18,1},{19,0},{4,23},{5,... | collective-permute-start | bytes 230408 | tf_op jit(solution)/shard_map/ppermute | solution.py:244
  88.0 9.1 %collective-permute-start.7 = (bf16[1,38400]{1,0:T(2,128)(2,1)S(1)}, bf16[1,38400]{1,0:T(2,128)(2,1)S(1)}, u32[]{:S(2)}, u32[]{:S(2)}) collective-permute-start(bf16[1,38400]{1,0:T(2,128)(2,1)S(1)} %get-tuple-element.14), channel_id=1, source_target_pairs={{0,18},{1,19},{2,16},{3,17},{16,2},{17,3},{18,0},{19,1},{4,22},{5,... | collective-permute-start | bytes 230408 | tf_op jit(solution)/shard_map/ppermute | solution.py:244
  90.3 8.6 %collective-permute-start.6 = (bf16[1,38400]{1,0:T(2,128)(2,1)S(1)}, bf16[1,38400]{1,0:T(2,128)(2,1)S(1)}, u32[]{:S(2)}, u32[]{:S(2)}) collective-permute-start(bf16[1,38400]{1,0:T(2,128)(2,1)S(1)} %get-tuple-element.15), channel_id=1, source_target_pairs={{0,17},{1,16},{2,19},{3,18},{16,1},{17,0},{18,3},{19,2},{4,21},{5,... | collective-permute-start | bytes 230408 | tf_op jit(solution)/shard_map/ppermute | solution.py:244
  90.4 12.2 %collective-permute-start.5 = (bf16[1,38400]{1,0:T(2,128)(2,1)S(1)}, bf16[1,38400]{1,0:T(2,128)(2,1)S(1)}, u32[]{:S(2)}, u32[]{:S(2)}) collective-permute-start(bf16[1,38400]{1,0:T(2,128)(2,1)S(1)} %get-tuple-element.16), channel_id=1, source_target_pairs={{0,16},{1,17},{2,18},{3,19},{16,0},{17,1},{18,2},{19,3},{4,20},{5,... | collective-permute-start | bytes 230408 | tf_op jit(solution)/shard_map/ppermute | solution.py:244
  91.0 11.6 %collective-permute-start.4 = (bf16[1,38400]{1,0:T(2,128)(2,1)S(1)}, bf16[1,38400]{1,0:T(2,128)(2,1)S(1)}, u32[]{:S(2)}, u32[]{:S(2)}) collective-permute-start(bf16[1,38400]{1,0:T(2,128)(2,1)S(1)} %get-tuple-element.17), channel_id=1, source_target_pairs={{0,3},{1,2},{2,1},{3,0},{16,19},{17,18},{18,17},{19,16},{4,7},{5,6... | collective-permute-start | bytes 230408 | tf_op jit(solution)/shard_map/ppermute | solution.py:244
  92.4 10.2 %collective-permute-start.3 = (bf16[1,38400]{1,0:T(2,128)(2,1)S(1)}, bf16[1,38400]{1,0:T(2,128)(2,1)S(1)}, u32[]{:S(2)}, u32[]{:S(2)}) collective-permute-start(bf16[1,38400]{1,0:T(2,128)(2,1)S(1)} %get-tuple-element.18), channel_id=1, source_target_pairs={{0,2},{1,3},{2,0},{3,1},{16,18},{17,19},{18,16},{19,17},{4,6},{5,7... | collective-permute-start | bytes 230408 | tf_op jit(solution)/shard_map/ppermute | solution.py:244
  97.1 5.5 %collective-permute-start.2 = (bf16[1,38400]{1,0:T(2,128)(2,1)S(1)}, bf16[1,38400]{1,0:T(2,128)(2,1)S(1)}, u32[]{:S(2)}, u32[]{:S(2)}) collective-permute-start(bf16[1,38400]{1,0:T(2,128)(2,1)S(1)} %get-tuple-element.19), channel_id=1, source_target_pairs={{0,1},{1,0},{2,3},{3,2},{16,17},{17,16},{18,19},{19,18},{4,5},{5,4... | collective-permute-start | bytes 230408 | tf_op jit(solution)/shard_map/ppermute | solution.py:244
  105.5 1.2 copy-start
  106.7 4.9 %slice-start = ((bf16[8,38400]{1,0:T(8,128)(2,1)}), bf16[8,13824]{1,0:T(8,128)(2,1)S(1)}, s32[]{:S(2)}) async-start(bf16[8,38400]{1,0:T(8,128)(2,1)} %copy-done), calls=%async_computation.1 | async-start | bytes 442368 | tf_op jit(solution)/shard_map/slice | solution.py:248
  107.1 10.2 %collective-permute-start.11 = (f32[4,2,2,32,32]{4,3,2,1,0:T(8,128)S(1)}, f32[4,2,2,32,32]{4,3,2,1,0:T(8,128)S(1)}, u32[]{:S(2)}, u32[]{:S(2)}) collective-permute-start(f32[4,2,2,32,32]{4,3,2,1,0:T(8,128)S(1)} %fusion.50), channel_id=1, source_target_pairs={{0,12},{4,0},{8,4},{12,8},{1,13},{5,1},{9,5},{13,9},{2,14},{6,2},{... | collective-permute-start | bytes 196616 | tf_op jit(solution)/shard_map/ppermute | solution.py:156
  110.5 22.2 %collective-permute-start.10 = (f32[4,2,2,32,32]{4,3,2,1,0:T(8,128)S(1)}, f32[4,2,2,32,32]{4,3,2,1,0:T(8,128)S(1)}, u32[]{:S(2)}, u32[]{:S(2)}) collective-permute-start(f32[4,2,2,32,32]{4,3,2,1,0:T(8,128)S(1)} %fusion.50), channel_id=1, source_target_pairs={{0,8},{4,12},{8,0},{12,4},{1,9},{5,13},{9,1},{13,5},{2,10},{6,14},... | collective-permute-start | bytes 196616 | tf_op jit(solution)/shard_map/ppermute | solution.py:156
  110.5 22.2 %collective-permute-start.9 = (f32[4,2,2,32,32]{4,3,2,1,0:T(8,128)S(1)}, f32[4,2,2,32,32]{4,3,2,1,0:T(8,128)S(1)}, u32[]{:S(2)}, u32[]{:S(2)}) collective-permute-start(f32[4,2,2,32,32]{4,3,2,1,0:T(8,128)S(1)} %fusion.50), channel_id=1, source_target_pairs={{0,4},{4,8},{8,12},{12,0},{1,5},{5,9},{9,13},{13,1},{2,6},{6,10},{... | collective-permute-start | bytes 196616 | tf_op jit(solution)/shard_map/ppermute | solution.py:156
  136.7 0.8 copy-start.3
Sparse Core Ops, SparseCore 0:
  19.1 51.9 all-reduce.2
